TPU v7x, 512 devices: a whole 4x8x8 slice. The times are simulated.
512 devices in a mesh: src: 32 (over y, x_lo, core), rcv: 8 (over z), int: 2 (over x_hi).
Axes of the slice: x: 4 (x_hi: 2, x_lo: 2; x = x_hi * 2 + x_lo), y: 8, z: 8, core: 2. Of those that a mesh axis runs over, the one named last changes fastest.
Arguments:
- traces: float32 [2, 1, 4096, 4096], P(None, None, 'src', 'rcv'), may hold values from -6 to 6
- missing: int32 [32, 32], P('src', 'rcv'), may hold values from 0 to 1, as said below
- aperture: int32 [32, 24], P('src'), may hold values from 0 to 32, as said below
- wavelet: float32 [2, 1], replicated, may hold values from -0.06 to 0.06
Outputs:
- primaries: float32 [2, 1, 4096, 4096], P(None, None, 'src', ('rcv', 'int'))
Inputs may be any that keep to these rules, and one draw needn't show every extreme that they name: `missing`: A tile is marked only where its receiver block lies above its source block, so the mirrored tile is always recorded; some tile is marked. `aperture`: in each row the listed blocks come first and are distinct; the remaining entries are the padding value 32. Each row lists 24 // 2 to 24 blocks; some row lists exactly 24 and some row exactly 12.
All inputs are finite; a program needn't handle non-finite values.
Results may differ from a plain program's by a relative error of at most 0.00005.
Values sent between devices are 32-bit elements; how exact they have to be, the bound alone decides.
No kernel may reach another device: no remote copies, remote signals or barrier semaphores. Data moves between devices by JAX's collectives and lax.ppermute only.
A program may use at most 64 MiB of HBM per device.

v0:
```python
import jax
import jax.numpy as jnp
from jax import lax
from jax.sharding import PartitionSpec as P

TILE = 128


def from_everyone(x, axis):
    copies = jnp.broadcast_to(x, (lax.axis_size(axis), *x.shape))
    return lax.all_to_all(copies, axis, split_axis=0, concat_axis=0, tiled=True)


def joined_along(pieces, dim):
    pieces = jnp.moveaxis(pieces, 0, dim)
    lengths = pieces.shape
    return pieces.reshape(*lengths[:dim], lengths[dim] * lengths[dim + 1], *lengths[dim + 2 :])


def collect(x, axis, dim):
    pieces = from_everyone(x, axis)
    return joined_along(pieces, dim)


def in_blocks(x, dim, count):
    before, after = (x.shape[:dim], x.shape[dim + 1 :])
    return jnp.moveaxis(x.reshape(*before, count, -1, *after), dim, 0)


def sent_and_summed(x, axis, dim):
    pieces = in_blocks(x, dim, lax.axis_size(axis))
    arrived = lax.all_to_all(pieces, axis, split_axis=0, concat_axis=0, tiled=True)
    return arrived.sum(axis=0)


def complex_prod(left_side, right_side):
    return jnp.einsum("fik,fkj->fij", left_side, right_side, precision=lax.Precision.HIGHEST)


def per_device(traces, missing, aperture, wavelet):
    half_count = lax.axis_size("int")
    my_half = lax.axis_index("int")
    rcv_count = lax.axis_size("rcv")
    comp_count, freq_count, local_rows, local_cols = traces.shape
    regrouped = lax.all_to_all(traces, "rcv", split_axis=2, concat_axis=3, tiled=True)
    sectioned = regrouped.reshape(
        comp_count, freq_count, 1, local_rows // rcv_count, local_cols * rcv_count
    )
    arrived = lax.all_to_all(
        lax.all_to_all(sectioned, "src", split_axis=4, concat_axis=2, tiled=True),
        "rcv",
        split_axis=2,
        concat_axis=3,
        tiled=True,
    )
    mirrored = jnp.swapaxes(arrived.reshape(comp_count, freq_count, local_cols, local_rows), 2, 3)
    row_tiles = local_rows // TILE
    col_tiles = local_cols // TILE
    tile_mask = jnp.broadcast_to(
        missing[:, None, :, None] > 0, (row_tiles, TILE, col_tiles, TILE)
    ).reshape(local_rows, local_cols)
    filled = jnp.where(tile_mask[None, None], mirrored, traces)
    half_tile = TILE // half_count
    left_half = filled.reshape(comp_count, freq_count, local_rows, col_tiles, half_count, half_tile)
    left_half = lax.dynamic_index_in_dim(left_half, my_half, 4, keepdims=False)
    left_half = left_half.reshape(comp_count, freq_count, local_rows, col_tiles * half_tile)
    right_half = filled.reshape(
        comp_count, freq_count, row_tiles, half_count, half_tile, local_cols
    )
    right_half = lax.dynamic_index_in_dim(right_half, my_half, 3, keepdims=False)
    right_half = right_half.reshape(comp_count, freq_count, row_tiles * half_tile, local_cols)
    gathered = collect(left_half, "rcv", 3)
    block_count = gathered.shape[3] // half_tile
    chosen = (
        (aperture[:, :, None] == jnp.arange(block_count, dtype=jnp.int32)[None, None, :])
        .astype(jnp.float32)
        .sum(axis=1)
    )
    weighted = gathered.reshape(comp_count, freq_count, row_tiles, TILE, block_count, half_tile)
    weighted = (weighted * chosen[None, None, :, None, :, None]).reshape(
        comp_count, freq_count, local_rows, block_count * half_tile
    )
    slab_piece = lax.all_gather(right_half, "src", axis=2, tiled=True)
    real_part = complex_prod(weighted[0], slab_piece[0]) - complex_prod(weighted[1], slab_piece[1])
    imag_part = complex_prod(weighted[0], slab_piece[1]) + complex_prod(weighted[1], slab_piece[0])
    partial_sum = jnp.stack([real_part, imag_part])
    out_cols = local_cols // half_count
    my_share = sent_and_summed(partial_sum, "int", 3)
    kept_data = filled.reshape(comp_count, freq_count, local_rows, half_count, out_cols)
    kept_data = lax.dynamic_index_in_dim(kept_data, my_half, 3, keepdims=False)
    w_real = wavelet[0][:, None, None]
    w_imag = wavelet[1][:, None, None]
    out_real = kept_data[0] - (w_real * my_share[0] - w_imag * my_share[1])
    out_imag = kept_data[1] - (w_real * my_share[1] + w_imag * my_share[0])
    return jnp.stack([out_real, out_imag])


def solution(mesh):
    placed = (P(None, None, "src", "rcv"), P("src", "rcv"), P("src", None), P())
    return jax.shard_map(
        per_device,
        mesh=mesh,
        in_specs=placed,
        out_specs=P(None, None, "src", ("rcv", "int")),
        check_vma=False,
    )
```

profile of v0, /device:TPU:1, one launch (start us, length us, event | category | flops | bytes accessed | tf_op | source)
XLA Modules:
  0.0 221.6 jit_solution(6146417646936769049)
XLA Ops:
  6.5 1.4 copy.59
  8.0 26.7 %all_to_all.58 = f32[2,1,128,512]{3,0,1,2:T(2,128)S(1)} all-to-all(f32[2,1,128,512]{3,0,1,2:T(2,128)S(1)} %copy.59), channel_id=1, replica_groups=mesh['src'=32,'rcv'=8,'int'=2] {'rcv'}, dimensions={2} | all-to-all | bytes 1048576 | tf_op jit(solution)/shard_map/all_to_all | solution.py:45
  34.7 4.3 %copy.73 = f32[2,1,16,8,512]{2,0,4,3,1:T(2,128)} copy(f32[2,1,16,8,512]{4,2,3,0,1:T(8,128)S(1)} %bitcast.68) | data formatting | bytes 1048576 | tf_op jit(solution)/shard_map/reshape | solution.py:46
  39.0 7.3 %reshape.263 = f32[32,1,4096]{2,1,0:T(1,128)S(1)} reshape(f32[4096,1,1,2,16]{4,3,2,1,0:T(2,128)} %bitcast.59) | data formatting | bytes 1048576
  46.4 27.2 %all_to_all.59 = f32[32,1,4096]{2,1,0:T(1,128)S(1)} all-to-all(f32[32,1,4096]{2,1,0:T(1,128)S(1)} %reshape.263), channel_id=1, replica_groups=mesh['src'=32,'rcv'=8,'int'=2] {'src'}, dimensions={0} | all-to-all | bytes 1048576 | tf_op jit(solution)/shard_map/all_to_all | solution.py:50
  74.0 1.9 reduce.2
  75.9 6.9 %reshape.264 = f32[4096,1,1,2,16]{4,3,2,1,0:T(2,128)} reshape(f32[32,4096]{1,0:T(8,128)S(1)} %reduce.2) | data formatting | bytes 1048576
  82.9 5.9 %copy.63 = f32[2,1,1,16,32,128]{5,3,0,4,2,1:T(8,128)} copy(f32[2,1,1,16,32,128]{3,0,5,4,2,1:T(2,128)} %bitcast.60) | data formatting | bytes 1048576 | tf_op jit(solution)/shard_map/all_to_all | solution.py:50
  88.7 3.5 %all-to-all-start.2 = ((f32[2,1,32,16,128]{4,3,0,1,2:T(8,128)}), f32[2,1,32,16,128]{4,3,0,1,2:T(8,128)S(1)}, u32[]{:S(2)}, u32[]{:S(2)}) async-start(f32[2,1,32,16,128]{4,3,0,1,2:T(8,128)} %bitcast.7), calls=%async_computation.2 | async-start | bytes 1048576 | tf_op jit(solution)/shard_map/all_to_all | solution.py:49
  92.6 15.9 %all-to-all-done.2 = f32[2,1,32,16,128]{4,3,0,1,2:T(8,128)S(1)} async-done(((f32[2,1,32,16,128]{4,3,0,1,2:T(8,128)}), f32[2,1,32,16,128]{4,3,0,1,2:T(8,128)S(1)}, u32[]{:S(2)}, u32[]{:S(2)}) %all-to-all-start.2) | async-done | bytes 524320 | tf_op jit(solution)/shard_map/all_to_all | solution.py:49
  108.9 0.7 constant_dynamic-slice_fusion.1
  109.7 1.6 broadcast_in_dim.25
  111.3 3.8 %all-to-all-start.3 = ((f32[8,2,1,128,256]{3,4,1,2,0:T(8,128)}), f32[8,2,1,128,256]{3,4,1,2,0:T(8,128)S(1)}, u32[]{:S(2)}, u32[]{:S(2)}) async-start(f32[8,2,1,128,256]{3,4,1,2,0:T(8,128)} %broadcast_in_dim.25), calls=%async_computation.3 | async-start | bytes 4194304 | tf_op jit(solution)/shard_map/all_to_all | solution.py:11
  115.2 48.5 %all-to-all-done.3 = f32[8,2,1,128,256]{3,4,1,2,0:T(8,128)S(1)} async-done(((f32[8,2,1,128,256]{3,4,1,2,0:T(8,128)}), f32[8,2,1,128,256]{3,4,1,2,0:T(8,128)S(1)}, u32[]{:S(2)}, u32[]{:S(2)}) %all-to-all-start.3) | async-done | bytes 2097184 | tf_op jit(solution)/shard_map/all_to_all | solution.py:11
  164.3 14.9 %all-gather.3.cloned.1.call-done = f32[2,1,1,1,2048,512]{5,4,3,0,2,1:T(8,128)} async-done(((f32[2,1,1,1,64,512]{5,4,3,0,2,1:T(8,128)}), f32[2,1,1,1,2048,512]{5,4,3,0,2,1:T(8,128)}) %all-gather.3.cloned.1.call-update) | async-done | bytes 8388624 | tf_op jit(solution)/shard_map/all_gather | solution.py:83
  179.2 4.8 %fusion = f32[128,512]{1,0:T(8,128)S(1)} fusion(f32[128,2048]{0,1:T(8,128)S(1)} %bitcast.61, f32[2,1,1,1,2048,512]{5,4,3,0,2,1:T(8,128)} %all-gather.3.cloned.1.call-done), kind=kOutput, calls=%fused_computation.2 | convolution fusion | flops 1610612736 | bytes 5505024 | tf_op jit(solution)/shard_map/fik,fkj->fij/dot_general | solution.py:37
  184.0 4.8 %fusion.5 = f32[128,512]{1,0:T(8,128)S(1)} fusion(f32[128,512]{1,0:T(8,128)S(1)} %fusion, f32[128,2048]{0,1:T(8,128)S(1)} %bitcast.63, f32[2,1,1,1,2048,512]{5,4,3,0,2,1:T(8,128)} %all-gather.3.cloned.1.call-done), kind=kOutput, calls=%fused_computation.7 | convolution fusion | flops 1610678272 | bytes 5767168 | tf_op jit(solution)/shard_map/fik,fkj->fij/dot_general | solution.py:37
  189.0 4.8 %fusion.1 = f32[128,512]{1,0:T(8,128)S(1)} fusion(f32[128,2048]{0,1:T(8,128)S(1)} %bitcast.64, f32[2,1,1,1,2048,512]{5,4,3,0,2,1:T(8,128)} %all-gather.3.cloned.1.call-done), kind=kOutput, calls=%fused_computation.3 | convolution fusion | flops 1610612736 | bytes 5505024 | tf_op jit(solution)/shard_map/fik,fkj->fij/dot_general | solution.py:37
  193.8 4.8 %fusion.4 = f32[128,512]{1,0:T(8,128)S(1)} fusion(f32[128,512]{1,0:T(8,128)S(1)} %fusion.1, f32[128,2048]{0,1:T(8,128)S(1)} %bitcast.62, f32[2,1,1,1,2048,512]{5,4,3,0,2,1:T(8,128)} %all-gather.3.cloned.1.call-done), kind=kOutput, calls=%fused_computation.6 | convolution fusion | flops 1610678272 | bytes 5767168 | tf_op jit(solution)/shard_map/fik,fkj->fij/dot_general | solution.py:37
  198.8 0.8 maximum_bitcast_fusion
  199.6 4.0 %all-to-all-start.4 = ((f32[2,2,1,128,256]{4,3,2,1,0:T(8,128)}), f32[2,2,1,128,256]{4,3,2,1,0:T(8,128)S(1)}, u32[]{:S(2)}, u32[]{:S(2)}) async-start(f32[2,2,1,128,256]{4,3,2,1,0:T(8,128)} %maximum_bitcast_fusion), calls=%async_computation.4 | async-start | bytes 1048576 | tf_op jit(solution)/shard_map/all_to_all | solution.py:32
  204.5 8.2 %all-to-all-done.4 = f32[2,2,1,128,256]{4,3,2,1,0:T(8,128)S(1)} async-done(((f32[2,2,1,128,256]{4,3,2,1,0:T(8,128)}), f32[2,2,1,128,256]{4,3,2,1,0:T(8,128)S(1)}, u32[]{:S(2)}, u32[]{:S(2)}) %all-to-all-start.4) | async-done | bytes 524320 | tf_op jit(solution)/shard_map/all_to_all | solution.py:32
  212.7 1.3 bitcast_subtract_fusion.1
  214.0 0.7 pad_maximum_fusion
  (33 shorter events, 3.3 us)
Async XLA Ops:
  75.9 16.3 %copy-start = (f32[2,1,128,512]{3,2,1,0:T(8,128)S(1)}, f32[2,1,128,512]{3,2,1,0:T(8,128)}, u32[]{:S(2)}) copy-start(f32[2,1,128,512]{3,2,1,0:T(8,128)} %param.4) | copy-start | bytes 1572868
  82.9 9.6 %copy-start.2 = (s32[1,4]{1,0:T(1,128)S(1)}, s32[1,4]{1,0:T(1,128)}, u32[]{:S(2)}) copy-start(s32[1,4]{1,0:T(1,128)} %param.5) | copy-start | bytes 52
  88.7 19.8 %all-to-all-start.2 = ((f32[2,1,32,16,128]{4,3,0,1,2:T(8,128)}), f32[2,1,32,16,128]{4,3,0,1,2:T(8,128)S(1)}, u32[]{:S(2)}, u32[]{:S(2)}) async-start(f32[2,1,32,16,128]{4,3,0,1,2:T(8,128)} %bitcast.7), calls=%async_computation.2 | async-start | bytes 1048576 | tf_op jit(solution)/shard_map/all_to_all | solution.py:49
  92.2 87.0 %all-gather.3.cloned.1.call-start = ((), (), s32[]{:S(2)}) async-start(), calls=%async_computation.5 | async-start | bytes 8650752 | tf_op jit(solution)/shard_map/all_gather | solution.py:83
  108.9 6.2 %copy-start.3 = (s32[1,24]{1,0:T(1,128)S(1)}, s32[1,24]{1,0:T(1,128)}, u32[]{:S(2)}) copy-start(s32[1,24]{1,0:T(1,128)} %param.6) | copy-start | bytes 292
  111.3 52.4 %all-to-all-start.3 = ((f32[8,2,1,128,256]{3,4,1,2,0:T(8,128)}), f32[8,2,1,128,256]{3,4,1,2,0:T(8,128)S(1)}, u32[]{:S(2)}, u32[]{:S(2)}) async-start(f32[8,2,1,128,256]{3,4,1,2,0:T(8,128)} %broadcast_in_dim.25), calls=%async_computation.3 | async-start | bytes 4194304 | tf_op jit(solution)/shard_map/all_to_all | solution.py:11
  193.8 9.8 %copy-start.1 = (f32[2,1]{0,1:T(1,128)S(1)}, f32[2,1]{0,1:T(1,128)}, u32[]{:S(2)}) copy-start(f32[2,1]{0,1:T(1,128)} %param.7) | copy-start | bytes 28
  199.6 13.0 %all-to-all-start.4 = ((f32[2,2,1,128,256]{4,3,2,1,0:T(8,128)}), f32[2,2,1,128,256]{4,3,2,1,0:T(8,128)S(1)}, u32[]{:S(2)}, u32[]{:S(2)}) async-start(f32[2,2,1,128,256]{4,3,2,1,0:T(8,128)} %maximum_bitcast_fusion), calls=%async_computation.4 | async-start | bytes 1048576 | tf_op jit(solution)/shard_map/all_to_all | solution.py:32
Sparse Core Ops, SparseCore 0:
  109.8 69.3 all-gather.2
where the time goes:
time: 222 us
  waiting for transfers between devices  87.5 us (39%)
  blocking collectives  53.8 us (24%)
  local copies, waits for them, and re-layouts  30.9 us (14%)
  matrix products  19.2 us (9%)
  between operations  13.7 us (6%)
  starting transfers between devices  11.3 us (5%)
  other arithmetic  5.23 us (2%)
    all_to_all x1, waiting for transfers between devices, from_everyone(): return lax.all_to_all(copies, axis, split_axis=0, concat_axis=0, tiled=True)  48.5 us
    all_to_all x1, blocking collectives, per_device(): lax.all_to_all(sectioned, 'src', split_axis=4, concat_axis=2, tiled=True)  27.2 us
    all_to_all x1, blocking collectives, per_device(): lax.all_to_all(traces, 'rcv', split_axis=2, concat_axis=3, tiled=True)  26.7 us
    dot_general x4, matrix products, complex_prod(): jnp.einsum('fik,fkj->fij', left_side, right_side, precision=lax.Precision...  19.2 us
    unnamed x14, local copies, waits for them, and re-layouts  16.1 us
    all_to_all x1, waiting for transfers between devices, per_device(): lax.all_to_all(lax.all_to_all(sectioned, 'src', split_axis=4, concat_axis...  15.9 us
    all_gather x1, waiting for transfers between devices, per_device(): slab_piece = lax.all_gather(right_half, 'src', axis=2, tiled=True)  14.9 us
    all_to_all x1, waiting for transfers between devices, sent_and_summed(): lax.all_to_all(pieces, axis, split_axis=0, concat_axis=0, tiled=True)  8.19 us
  transfers between devices with their start and end apart: 4, of which 4 were waited for; matrix products, arithmetic and copies ran while one was open for 2% of the time, Pallas kernels for 0%

commit v1 on v0

--- a/solution.py
+++ b/solution.py
@@ -80,7 +80,8 @@
     weighted = (weighted * chosen[None, None, :, None, :, None]).reshape(
         comp_count, freq_count, local_rows, block_count * half_tile
     )
-    slab_piece = lax.all_gather(right_half, "src", axis=2, tiled=True)
+    sent = jnp.stack([right_half] * lax.axis_size("src"))
+    slab_piece = jnp.concatenate(lax.all_to_all(sent, "src", 0, 0), axis=2)
     real_part = complex_prod(weighted[0], slab_piece[0]) - complex_prod(weighted[1], slab_piece[1])
     imag_part = complex_prod(weighted[0], slab_piece[1]) + complex_prod(weighted[1], slab_piece[0])
     partial_sum = jnp.stack([real_part, imag_part])

time: 222 us -> 389 us (1.75)
  waiting for transfers between devices: 87.5 us -> 261 us
  between operations: 13.7 us -> 0.31 us
  local copies, waits for them, and re-layouts: 30.9 us -> 39 us
  matrix products: 19.2 us -> 12.8 us
  starting transfers between devices: 11.3 us -> 16.2 us
    all_to_all x0 -> x1, waiting for transfers between devices: none -> 186 us  [per_device(): slab_piece = jnp.concatenate(lax.all_to_all(sent, 'src', 0, 0), axis=2)]
    all_gather x1 -> x0, waiting for transfers between devices: 14.9 us -> none  [per_device(): slab_piece = lax.all_gather(right_half, 'src', axis=2, tiled=True)]
    dot_general x4, matrix products: 19.2 us -> 12.8 us  [complex_prod(): jnp.einsum('fik,fkj->fij', left_side, right_side, precision=lax.Precision...]
    all_to_all x0 -> x1, starting transfers between devices: none -> 5.4 us  [per_device(): slab_piece = jnp.concatenate(lax.all_to_all(sent, 'src', 0, 0), axis=2)]
    slice x1 -> x2, local copies, waits for them, and re-layouts: 0.24 us -> 4.77 us  [the longest x1 4.53 us: per_device(): slab_piece[0]]
    another operation x0 -> x2, local copies, waits for them, and re-layouts: none -> 4.33 us  [per_device(): sent = jnp.stack([right_half] * lax.axis_size('src'))]
    unnamed x14 -> x16, local copies, waits for them, and re-layouts: 16.1 us -> 16.1 us
  transfers between devices with their start and end apart: 4 -> 4, of which waited for: 4 -> 4; matrix products, arithmetic and copies ran while one was open for 2% -> 1% of each run, Pallas kernels for 0% -> 0%
where the time goes in v1:
time: 389 us; the launch traced here: 388 us
  waiting for transfers between devices  261 us (67%)
  blocking collectives  53.8 us (14%)
  local copies, waits for them, and re-layouts  39 us (10%)
  starting transfers between devices  16.2 us (4%)
  matrix products  12.8 us (3%)
  other arithmetic  5.24 us (1%)
    all_to_all x1, waiting for transfers between devices, per_device(): slab_piece = jnp.concatenate(lax.all_to_all(sent, 'src', 0, 0), axis=2)  186 us
    all_to_all x1, waiting for transfers between devices, from_everyone(): return lax.all_to_all(copies, axis, split_axis=0, concat_axis=0, tiled=True)  51.3 us
    all_to_all x1, blocking collectives, per_device(): lax.all_to_all(sectioned, 'src', split_axis=4, concat_axis=2, tiled=True)  27.2 us
    all_to_all x1, blocking collectives, per_device(): lax.all_to_all(traces, 'rcv', split_axis=2, concat_axis=3, tiled=True)  26.7 us
    unnamed x16, local copies, waits for them, and re-layouts  16.1 us
    all_to_all x1, waiting for transfers between devices, per_device(): lax.all_to_all(lax.all_to_all(sectioned, 'src', split_axis=4, concat_axis...  16 us
    dot_general x4, matrix products, complex_prod(): jnp.einsum('fik,fkj->fij', left_side, right_side, precision=lax.Precision...  12.8 us
    all_to_all x1, waiting for transfers between devices, sent_and_summed(): lax.all_to_all(pieces, axis, split_axis=0, concat_axis=0, tiled=True)  7.98 us
  transfers between devices with their start and end apart: 4, of which 4 were waited for; matrix products, arithmetic and copies ran while one was open for 1% of the time, Pallas kernels for 0%

profile of v1, /device:TPU:1, one launch (start us, length us, event | category | flops | bytes accessed | tf_op | source)
XLA Modules:
  0.0 388.4 jit_solution(4078978380341721298)
XLA Ops:
  0.0 1.4 copy.59
  1.4 26.7 %all_to_all.63 = f32[2,1,128,512]{3,0,1,2:T(2,128)S(1)} all-to-all(f32[2,1,128,512]{3,0,1,2:T(2,128)S(1)} %copy.59), channel_id=1, replica_groups=mesh['src'=32,'rcv'=8,'int'=2] {'rcv'}, dimensions={2} | all-to-all | bytes 1048576 | tf_op jit(solution)/shard_map/all_to_all | solution.py:45
  28.2 4.3 %copy.73 = f32[2,1,16,8,512]{2,0,4,3,1:T(2,128)} copy(f32[2,1,16,8,512]{4,2,3,0,1:T(8,128)S(1)} %bitcast.69) | data formatting | bytes 1048576 | tf_op jit(solution)/shard_map/reshape | solution.py:46
  32.5 7.3 %reshape.267 = f32[32,1,4096]{2,1,0:T(1,128)S(1)} reshape(f32[4096,1,1,2,16]{4,3,2,1,0:T(2,128)} %bitcast.60) | data formatting | bytes 1048576
  39.8 27.2 %all_to_all.64 = f32[32,1,4096]{2,1,0:T(1,128)S(1)} all-to-all(f32[32,1,4096]{2,1,0:T(1,128)S(1)} %reshape.267), channel_id=1, replica_groups=mesh['src'=32,'rcv'=8,'int'=2] {'src'}, dimensions={0} | all-to-all | bytes 1048576 | tf_op jit(solution)/shard_map/all_to_all | solution.py:50
  67.5 1.9 reduce.2
  69.4 6.9 %reshape.268 = f32[4096,1,1,2,16]{4,3,2,1,0:T(2,128)} reshape(f32[32,4096]{1,0:T(8,128)S(1)} %reduce.2) | data formatting | bytes 1048576
  76.3 5.8 %copy.63 = f32[2,1,1,16,32,128]{5,3,0,4,2,1:T(8,128)} copy(f32[2,1,1,16,32,128]{3,0,5,4,2,1:T(2,128)} %bitcast.61) | data formatting | bytes 1048576 | tf_op jit(solution)/shard_map/all_to_all | solution.py:50
  82.2 3.5 all-to-all-start.2
  86.0 16.0 %all-to-all-done.2 = f32[2,1,32,16,128]{4,3,0,1,2:T(8,128)S(1)} async-done(((f32[2,1,32,16,128]{4,3,0,1,2:T(8,128)}), f32[2,1,32,16,128]{4,3,0,1,2:T(8,128)S(1)}, u32[]{:S(2)}, u32[]{:S(2)}) %all-to-all-start.2) | async-done | bytes 524320 | tf_op jit(solution)/shard_map/all_to_all | solution.py:49
  102.2 1.5 broadcast_in_dim.25
  103.8 3.6 all-to-all-start.3
  107.6 51.3 %all-to-all-done.3 = f32[8,2,1,128,256]{3,4,1,2,0:T(8,128)S(1)} async-done(((f32[8,2,1,128,256]{3,4,1,2,0:T(8,128)}), f32[8,2,1,128,256]{3,4,1,2,0:T(8,128)S(1)}, u32[]{:S(2)}, u32[]{:S(2)}) %all-to-all-start.3) | async-done | bytes 2097184 | tf_op jit(solution)/shard_map/all_to_all | solution.py:11
  159.0 4.3 %stack.17 = f32[32,2,1,64,512]{4,3,2,1,0:T(8,128)} broadcast(f32[2,64,512]{2,1,0:T(8,128)S(1)} %dynamic-slice_bitcast_fusion), dimensions={1,3,4} | broadcast | bytes 8650752 | tf_op jit(solution)/shard_map/stack | solution.py:83
  163.3 5.4 %all-to-all-start.4 = ((f32[32,2,1,64,512]{4,3,2,1,0:T(8,128)}), f32[32,2,1,64,512]{4,3,2,1,0:T(8,128)}, u32[]{:S(2)}, u32[]{:S(2)}) async-start(f32[32,2,1,64,512]{4,3,2,1,0:T(8,128)} %stack.17), calls=%async_computation.4 | async-start | bytes 16777216 | tf_op jit(solution)/shard_map/all_to_all | solution.py:84
  169.4 185.8 %all-to-all-done.4 = f32[32,2,1,64,512]{4,3,2,1,0:T(8,128)} async-done(((f32[32,2,1,64,512]{4,3,2,1,0:T(8,128)}), f32[32,2,1,64,512]{4,3,2,1,0:T(8,128)}, u32[]{:S(2)}, u32[]{:S(2)}) %all-to-all-start.4) | async-done | bytes 8388640 | tf_op jit(solution)/shard_map/all_to_all | solution.py:84
  355.2 4.5 %fusion = (f32[1,1,32,64,512]{4,3,1,0,2:T(8,128)S(1)}, f32[1,1,32,64,512]{4,3,1,0,2:T(8,128)S(1)}) fusion(f32[2,1,32,64,512]{4,3,1,0,2:T(8,128)} %bitcast.23), kind=kLoop, calls=%fused_computation.16 | loop fusion | bytes 16777216 | tf_op jit(solution)/shard_map/slice | solution.py:85
  359.7 2.7 fusion.3
  362.4 2.7 fusion.4
  365.1 2.7 convolution_subtract_fusion
  368.0 4.8 %convolution_add_fusion = f32[128,512]{1,0:T(8,128)S(1)} fusion(f32[128,512]{1,0:T(8,128)S(1)} %fusion.4, f32[128,2048]{0,1:T(8,128)S(1)} %bitcast.63, f32[2048,512]{1,0:T(8,128)} %bitcast.57), kind=kOutput, calls=%fused_computation | convolution fusion | flops 1610678272 | bytes 5767168 | tf_op jit(solution)/shard_map/fik,fkj->fij/dot_general | solution.py:37
  373.8 3.7 all-to-all-start.5
  378.4 8.0 %all-to-all-done.5 = f32[2,2,1,128,256]{4,3,2,1,0:T(8,128)S(1)} async-done(((f32[2,2,1,128,256]{4,3,2,1,0:T(8,128)}), f32[2,2,1,128,256]{4,3,2,1,0:T(8,128)S(1)}, u32[]{:S(2)}, u32[]{:S(2)}) %all-to-all-start.5) | async-done | bytes 524320 | tf_op jit(solution)/shard_map/all_to_all | solution.py:32
  386.4 1.3 bitcast_subtract_fusion.1
  (36 shorter events, 4.8 us)
Async XLA Ops:
  69.4 16.3 %copy-start.1 = (f32[2,1,128,512]{3,2,1,0:T(8,128)S(1)}, f32[2,1,128,512]{3,2,1,0:T(8,128)}, u32[]{:S(2)}) copy-start(f32[2,1,128,512]{3,2,1,0:T(8,128)} %param.4) | copy-start | bytes 1572868
  76.3 9.6 %copy-start.3 = (s32[1,4]{1,0:T(1,128)S(1)}, s32[1,4]{1,0:T(1,128)}, u32[]{:S(2)}) copy-start(s32[1,4]{1,0:T(1,128)} %param.5) | copy-start | bytes 52
  82.2 19.8 %all-to-all-start.2 = ((f32[2,1,32,16,128]{4,3,0,1,2:T(8,128)}), f32[2,1,32,16,128]{4,3,0,1,2:T(8,128)S(1)}, u32[]{:S(2)}, u32[]{:S(2)}) async-start(f32[2,1,32,16,128]{4,3,0,1,2:T(8,128)} %bitcast.7), calls=%async_computation.2 | async-start | bytes 1048576 | tf_op jit(solution)/shard_map/all_to_all | solution.py:49
  103.8 55.2 %all-to-all-start.3 = ((f32[8,2,1,128,256]{3,4,1,2,0:T(8,128)}), f32[8,2,1,128,256]{3,4,1,2,0:T(8,128)S(1)}, u32[]{:S(2)}, u32[]{:S(2)}) async-start(f32[8,2,1,128,256]{3,4,1,2,0:T(8,128)} %broadcast_in_dim.25), calls=%async_computation.3 | async-start | bytes 4194304 | tf_op jit(solution)/shard_map/all_to_all | solution.py:11
  163.3 5.4 %copy-start.4 = (s32[1,24]{1,0:T(1,128)S(1)}, s32[1,24]{1,0:T(1,128)}, u32[]{:S(2)}) copy-start(s32[1,24]{1,0:T(1,128)} %param.6) | copy-start | bytes 292
  163.3 191.9 %all-to-all-start.4 = ((f32[32,2,1,64,512]{4,3,2,1,0:T(8,128)}), f32[32,2,1,64,512]{4,3,2,1,0:T(8,128)}, u32[]{:S(2)}, u32[]{:S(2)}) async-start(f32[32,2,1,64,512]{4,3,2,1,0:T(8,128)} %stack.17), calls=%async_computation.4 | async-start | bytes 16777216 | tf_op jit(solution)/shard_map/all_to_all | solution.py:84
  359.7 5.3 %copy-start = (f32[1,1,32,64,512]{4,3,1,0,2:T(8,128)}, f32[1,1,32,64,512]{4,3,1,0,2:T(8,128)S(1)}, u32[]{:S(2)}) copy-start(f32[1,1,32,64,512]{4,3,1,0,2:T(8,128)S(1)} %get-tuple-element.5) | copy-start | bytes 12582916
  368.0 9.6 %copy-start.2 = (f32[2,1]{0,1:T(1,128)S(1)}, f32[2,1]{0,1:T(1,128)}, u32[]{:S(2)}) copy-start(f32[2,1]{0,1:T(1,128)} %param.7) | copy-start | bytes 28
  373.8 12.5 %all-to-all-start.5 = ((f32[2,2,1,128,256]{4,3,2,1,0:T(8,128)}), f32[2,2,1,128,256]{4,3,2,1,0:T(8,128)S(1)}, u32[]{:S(2)}, u32[]{:S(2)}) async-start(f32[2,2,1,128,256]{4,3,2,1,0:T(8,128)} %maximum_bitcast_fusion), calls=%async_computation.5 | async-start | bytes 1048576 | tf_op jit(solution)/shard_map/all_to_all | solution.py:32
